TPU v7x, 256 devices: a whole 4x4x8 slice. The times are simulated.
256 devices in a mesh: dp: 64 (over x, z, core), tensor: 4 (over y).
Axes of the slice: x: 4, y: 4, z: 8, core: 2. Of those that a mesh axis runs over, the one named last changes fastest.
Arguments:
- attention_grads: bfloat16 [64, 1, 512, 2048], P('dp', None, None, 'tensor')
- expert_grads: bfloat16 [64, 1, 2, 512, 4096], P('dp', None, None, None, 'tensor')
- routing_grads: bfloat16 [64, 4, 1, 36, 512], P('dp', 'tensor'), may hold values from -640 to 640
- attention_master: float32 [512, 2048], P('dp', 'tensor'), may hold values from -0.25 to 0.25
- attention_first: float32 [512, 2048], P('dp', 'tensor'), may hold values from -4 to 4
- attention_second: float32 [512, 2048], P('dp', 'tensor'), may hold values from 0.05 to 2
- expert_master: float32 [2, 512, 4096], P(None, 'dp', 'tensor'), may hold values from -0.25 to 0.25
- expert_first: float32 [2, 512, 4096], P(None, 'dp', 'tensor'), may hold values from -4 to 4
- expert_second: float32 [2, 512, 4096], P(None, 'dp', 'tensor'), may hold values from 0.05 to 2
- routing_master: float32 [36, 512], P(None, ('dp', 'tensor')), may hold values from -4 to 4
- routing_first: float32 [36, 512], P(None, ('dp', 'tensor')), may hold values from -4 to 4
- routing_second: float32 [36, 512], P(None, ('dp', 'tensor')), may hold values from 0.05 to 2
- step_count: int32 [1], replicated, may hold values from 1 to 1000
- learn_rate: float32 [1], replicated, may hold values from 0.05 to 0.3
- clip_level: float32 [1], replicated, may hold values from 0.5 to 2
Outputs:
- attention_renewed: float32 [512, 2048], P('dp', 'tensor')
- attention_momentum: float32 [512, 2048], P('dp', 'tensor')
- attention_variance: float32 [512, 2048], P('dp', 'tensor')
- attention_served: bfloat16 [512, 2048], P(None, 'tensor')
- expert_renewed: float32 [2, 512, 4096], P(None, 'dp', 'tensor')
- expert_momentum: float32 [2, 512, 4096], P(None, 'dp', 'tensor')
- expert_variance: float32 [2, 512, 4096], P(None, 'dp', 'tensor')
- expert_served: bfloat16 [2, 512, 4096], P(None, None, 'tensor')
- routing_renewed: float32 [36, 512], P(None, ('dp', 'tensor'))
- routing_momentum: float32 [36, 512], P(None, ('dp', 'tensor'))
- routing_variance: float32 [36, 512], P(None, ('dp', 'tensor'))
- routing_served: bfloat16 [36, 512], replicated
Inputs may be any that keep to these rules, and one draw needn't show every extreme that they name: `step_count`: the number of optimizer steps taken, this one included.
All inputs are finite; a program needn't handle non-finite values.
Results may differ from a plain program's by a relative error of at most 0.0004.
Values may be sent and summed in bfloat16 or wider, within the bound.
No kernel may reach another device: no remote copies, remote signals or barrier semaphores. Data moves between devices by JAX's collectives and lax.ppermute only.
A program may use at most 64 MiB of HBM per device.

v0:
```python
from functools import reduce
import jax
import jax.numpy as jnp
from jax import lax
from jax.sharding import PartitionSpec as P

EXPERTS = 32
PARAMS = 5261312
BETA_ONE = 0.9
BETA_TWO = 0.999
EPSILON = 1e-08
DECAY = 0.1


def micro_total(blocks):
    return reduce(lambda left, right: left + right, [blocks[0].astype(jnp.float32)])


def adam_update(grad_sum, master, first, second, clip, rate, first_fix, second_fix, mask):
    grad = clip * grad_sum
    momentum = BETA_ONE * first + (1.0 - BETA_ONE) * grad
    variance = BETA_TWO * second + (1.0 - BETA_TWO) * grad * grad
    update = (
        momentum / first_fix / (jnp.sqrt(variance / second_fix) + EPSILON) + DECAY * mask * master
    )
    renewed = master - rate * update
    return (renewed, momentum, variance, renewed.astype(jnp.bfloat16))


def local(
    attention_grads,
    expert_grads,
    routing_grads,
    attention_master,
    attention_first,
    attention_second,
    expert_master,
    expert_first,
    expert_second,
    routing_master,
    routing_first,
    routing_second,
    step_count,
    learn_rate,
    clip_level,
):
    attention_local = attention_grads[0]
    expert_local = expert_grads[0]
    attention_sum = lax.psum_scatter(
        micro_total(attention_local), "dp", scatter_dimension=0, tiled=True
    )
    expert_sum = lax.psum_scatter(micro_total(expert_local), "dp", scatter_dimension=1, tiled=True)
    expert_pieces = [expert_sum[index] for index in range(expert_sum.shape[0])]
    routing_local = micro_total(routing_grads[0, 0])
    routing_sum = lax.psum_scatter(routing_local, ("dp", "tensor"), scatter_dimension=1, tiled=True)
    expert_squares = reduce(
        lambda left, right: left + right, [jnp.sum(piece * piece) for piece in expert_pieces]
    )
    attention_total, expert_total, routing_total = lax.psum(
        (
            jnp.sum(attention_sum * attention_sum),
            expert_squares,
            jnp.sum(routing_sum * routing_sum),
        ),
        ("dp", "tensor"),
    )
    grad_norm = jnp.sqrt(attention_total + expert_total + routing_total)
    clip = jnp.minimum(1.0, clip_level[0] * jnp.sqrt(jnp.float32(PARAMS)) / (grad_norm + 1e-06))
    steps_done = step_count[0].astype(jnp.float32)
    first_fix = 1.0 - jnp.power(jnp.float32(BETA_ONE), steps_done)
    second_fix = 1.0 - jnp.power(jnp.float32(BETA_TWO), steps_done)
    rate = learn_rate[0]
    attention_out = adam_update(
        attention_sum,
        attention_master,
        attention_first,
        attention_second,
        clip,
        rate,
        first_fix,
        second_fix,
        jnp.float32(1.0),
    )
    attention_served = lax.all_gather(attention_out[3], "dp", axis=0, tiled=True)
    expert_sum = jnp.stack(expert_pieces, axis=0)
    expert_out = adam_update(
        expert_sum,
        expert_master,
        expert_first,
        expert_second,
        clip,
        rate,
        first_fix,
        second_fix,
        jnp.float32(1.0),
    )
    expert_renewed, expert_momentum, expert_variance = (expert_out[0], expert_out[1], expert_out[2])
    expert_served = lax.all_gather(expert_out[3], "dp", axis=1, tiled=True)
    row_index = jnp.arange(routing_master.shape[0], dtype=jnp.int32)
    routing_mask = (row_index < EXPERTS).astype(jnp.float32)[:, None]
    routing_out = adam_update(
        routing_sum,
        routing_master,
        routing_first,
        routing_second,
        clip,
        rate,
        first_fix,
        second_fix,
        routing_mask,
    )
    routing_served = lax.all_gather(routing_out[3], ("dp", "tensor"), axis=1, tiled=True)
    return (
        attention_out[0],
        attention_out[1],
        attention_out[2],
        attention_served,
        expert_renewed,
        expert_momentum,
        expert_variance,
        expert_served,
        routing_out[0],
        routing_out[1],
        routing_out[2],
        routing_served,
    )


def solution(mesh):
    in_specs = (
        P("dp", None, None, "tensor"),
        P("dp", None, None, None, "tensor"),
        P("dp", "tensor", None, None, None),
        P("dp", "tensor"),
        P("dp", "tensor"),
        P("dp", "tensor"),
        P(None, "dp", "tensor"),
        P(None, "dp", "tensor"),
        P(None, "dp", "tensor"),
        P(None, ("dp", "tensor")),
        P(None, ("dp", "tensor")),
        P(None, ("dp", "tensor")),
        P(),
        P(),
        P(),
    )
    out_specs = (
        P("dp", "tensor"),
        P("dp", "tensor"),
        P("dp", "tensor"),
        P(None, "tensor"),
        P(None, "dp", "tensor"),
        P(None, "dp", "tensor"),
        P(None, "dp", "tensor"),
        P(None, None, "tensor"),
        P(None, ("dp", "tensor")),
        P(None, ("dp", "tensor")),
        P(None, ("dp", "tensor")),
        P(),
    )
    return jax.shard_map(local, mesh=mesh, in_specs=in_specs, out_specs=out_specs, check_vma=False)
```

profile of v0, /device:TPU:1, one launch (start us, length us, event | category | flops | bytes accessed | tf_op | source)
XLA Modules:
  0.0 543.5 jit_solution(8500737560989414469)
XLA Ops:
  8.0 0.0 copy-start
  8.0 0.0 all-reduce.3.cloned.1.call-start
  8.1 1.1 copy.29
  9.1 0.7 bitcast_convert_fusion.2
  9.9 0.0 all-reduce.3.cloned.1.call-update
  9.9 0.0 reduce-scatter.3.cloned.1.call-start
  9.9 2.1 bitcast_convert_fusion.1
  12.1 0.0 reduce-scatter.3.cloned.1.call-update
  12.1 0.0 reduce-scatter.5.cloned.1.call-start
  12.2 2.4 bitcast_convert_fusion
  14.6 0.0 copy-start.8
  14.6 0.0 copy-start.9
  14.6 0.0 copy-start.4
  14.6 0.0 copy-start.5
  14.6 0.0 copy-start.6
  14.6 0.0 reduce-scatter.5.cloned.1.call-update
  14.7 0.0 all-gather.3.cloned.1.call-start
  16.8 256.6 %all-reduce.3.cloned.1.call-done = f32[36,512]{0,1:T(8,128)} async-done(((f32[36,512]{0,1:T(8,128)}), f32[36,512]{0,1:T(8,128)}) %all-reduce.3.cloned.1.call-update) | async-done | bytes 73744
  273.4 1.3 multiply_reduce_fusion.1
  274.7 1.3 multiply_reduce_fusion
  276.0 24.4 %reduce-scatter.5.cloned.1.call-done = f32[2,8,1024]{2,1,0:T(8,128)} async-done(((f32[2,512,1024]{2,1,0:T(8,128)}), f32[2,8,1024]{2,1,0:T(8,128)}) %reduce-scatter.5.cloned.1.call-update) | async-done | bytes 65552 | tf_op jit(solution)/shard_map/reduce_scatter | solution.py:52
  300.5 1.4 fusion.1
  304.5 79.6 %psum.25 = f32[]{:T(128)} all-reduce(f32[]{:T(128)S(6)} %add.71), channel_id=1, replica_groups=mesh['dp'=64,'tensor'=4] {'dp','tensor'}, use_global_device_ids=true, to_apply=%region_2.0 | all-reduce | flops 1 | bytes 8 | tf_op jit(solution)/shard_map/psum | solution.py:59
  384.9 1.5 fusion.6
  386.4 0.0 all-gather.3.cloned.1.call-update
  386.5 1.3 convert_bitcast_fusion
  387.8 93.8 %all-gather = bf16[256,2,36]{2,1,0:T(2,128)(2,1)S(1)} all-gather(bf16[1,2,36]{2,1,0:T(2,128)(2,1)S(1)} %get-tuple-element.14), channel_id=1, replica_groups=mesh['dp'=64,'tensor'=4] {'dp','tensor'}, dimensions={0}, use_global_device_ids=true | all-gather | bytes 37008 | tf_op jit(solution)/shard_map/all_gather | solution.py:112
  481.5 0.7 copy.30
  482.3 1.4 fusion.8
  483.6 48.4 %all_gather.9 = bf16[512,512]{1,0:T(8,128)(2,1)S(1)} all-gather(bf16[8,512]{1,0:T(8,128)(2,1)S(1)} %get-tuple-element.22), channel_id=1, replica_groups=mesh['dp'=64,'tensor'=4] {'dp'}, dimensions={0}, use_global_device_ids=true | all-gather | bytes 532480 | tf_op jit(solution)/shard_map/all_gather | solution.py:84
  532.1 0.8 copy.37
  532.9 3.1 copy.38
  (17 shorter events, 0.0 us)
Async XLA Ops:
  8.0 4.1 copy-start
  8.0 265.4 %all-reduce.3.cloned.1.call-start = ((), (), s32[]{:S(2)}) async-start(), calls=%async_computation.5 | async-start | bytes 524288
  9.9 264.8 %reduce-scatter.3.cloned.1.call-start = ((), (), s32[]{:S(2)}) async-start(), calls=%async_computation.2 | async-start | bytes 1064960 | tf_op jit(solution)/shard_map/reduce_scatter | solution.py:49
  12.1 288.4 %reduce-scatter.5.cloned.1.call-start = ((), (), s32[]{:S(2)}) async-start(), calls=%async_computation.3 | async-start | bytes 4259840 | tf_op jit(solution)/shard_map/reduce_scatter | solution.py:52
  14.6 370.3 %copy-start.1 = (f32[2,8,1024]{2,1,0:T(8,128)S(1)}, f32[2,8,1024]{2,1,0:T(8,128)}, u32[]{:S(2)}) copy-start(f32[2,8,1024]{2,1,0:T(8,128)} %param.21) | copy-start | bytes 196612
  14.6 370.3 %copy-start.2 = (f32[2,8,1024]{2,1,0:T(8,128)S(1)}, f32[2,8,1024]{2,1,0:T(8,128)}, u32[]{:S(2)}) copy-start(f32[2,8,1024]{2,1,0:T(8,128)} %param.23) | copy-start | bytes 196612
  14.6 370.3 %copy-start.3 = (f32[2,8,1024]{2,1,0:T(8,128)S(1)}, f32[2,8,1024]{2,1,0:T(8,128)}, u32[]{:S(2)}) copy-start(f32[2,8,1024]{2,1,0:T(8,128)} %param.22) | copy-start | bytes 196612
  14.6 371.9 %copy-start.7 = (f32[36,2]{0,1:T(2,128)S(1)}, f32[36,2]{0,1:T(2,128)}, u32[]{:S(2)}) copy-start(f32[36,2]{0,1:T(2,128)} %param.24) | copy-start | bytes 868
  14.6 371.9 %copy-start.8 = (f32[36,2]{0,1:T(2,128)S(1)}, f32[36,2]{0,1:T(2,128)}, u32[]{:S(2)}) copy-start(f32[36,2]{0,1:T(2,128)} %param.26) | copy-start | bytes 868
  14.6 371.9 %copy-start.9 = (f32[36,2]{0,1:T(2,128)S(1)}, f32[36,2]{0,1:T(2,128)}, u32[]{:S(2)}) copy-start(f32[36,2]{0,1:T(2,128)} %param.25) | copy-start | bytes 868
  14.6 467.7 %copy-start.4 = (f32[8,512]{1,0:T(8,128)S(1)}, f32[8,512]{1,0:T(8,128)}, u32[]{:S(2)}) copy-start(f32[8,512]{1,0:T(8,128)} %param.18) | copy-start | bytes 49156
  14.6 467.7 %copy-start.5 = (f32[8,512]{1,0:T(8,128)S(1)}, f32[8,512]{1,0:T(8,128)}, u32[]{:S(2)}) copy-start(f32[8,512]{1,0:T(8,128)} %param.20) | copy-start | bytes 49156
  14.6 467.7 %copy-start.6 = (f32[8,512]{1,0:T(8,128)S(1)}, f32[8,512]{1,0:T(8,128)}, u32[]{:S(2)}) copy-start(f32[8,512]{1,0:T(8,128)} %param.19) | copy-start | bytes 49156
  14.7 517.4 %all-gather.3.cloned.1.call-start = ((), (), s32[]{:S(2)}) async-start(), calls=%async_computation.4 | async-start | bytes 2129920 | tf_op jit(solution)/shard_map/all_gather | solution.py:98
Sparse Core Ops, SparseCore 0:
  14.9 258.5 all-reduce.2
Sparse Core Ops, SparseCore 1:
  14.9 139.2 reduce-scatter.2
  158.2 142.3 reduce-scatter.4
  386.5 74.5 all-gather.2
where the time goes:
time: 544 us
  waiting for transfers between devices  281 us (52%)
  blocking collectives  222 us (41%)
  between operations  21.2 us (4%)
  other arithmetic  13.5 us (2%)
  local copies, waits for them, and re-layouts  5.73 us (1%)
    unnamed x5, waiting for transfers between devices  257 us
    all_gather x1, blocking collectives, local(): lax.all_gather(routing_out[3], ('dp', 'tensor'), axis=1, tiled=True)  93.8 us
    psum x1, blocking collectives, local(): lax.psum((jnp.sum(attention_sum * attention_sum), expert_squares, jnp.sum...  79.6 us
    all_gather x1, blocking collectives, local(): lax.all_gather(attention_out[3], 'dp', axis=0, tiled=True)  48.4 us
    reduce_scatter x1, waiting for transfers between devices, local(): lax.psum_scatter(micro_total(expert_local), 'dp', scatter_dimension=1, ti...  24.4 us
  transfers between devices with their start and end apart: 4, of which 2 were waited for; matrix products, arithmetic and copies ran while one was open for 2% of the time, Pallas kernels for 0%

commit v1 on v0

--- a/solution.py
+++ b/solution.py
@@ -109,7 +109,12 @@
         second_fix,
         routing_mask,
     )
-    routing_served = lax.all_gather(routing_out[3], ("dp", "tensor"), axis=1, tiled=True)
+    field_in = routing_out[3]
+    far_arr = jax.lax.axis_size(("dp", "tensor"))
+    y1 = jnp.stack([field_in] * far_arr, 0)
+    routing_served = jnp.concatenate(
+        jax.lax.all_to_all(y1, ("dp", "tensor"), split_axis=0, concat_axis=0), 1
+    )
     return (
         attention_out[0],
         attention_out[1],

time: 544 us -> 473 us (0.87)
  blocking collectives: 222 us -> 132 us
  waiting for transfers between devices: 281 us -> 290 us
  starting transfers between devices: 0.17 us -> 8.75 us
    all_gather x1 -> x0, blocking collectives: 93.8 us -> none  [local(): lax.all_gather(routing_out[3], ('dp', 'tensor'), axis=1, tiled=True)]
    all_gather x1, waiting for transfers between devices: 0.01 us -> 9.16 us  [local(): expert_served = lax.all_gather(expert_out[3], 'dp', axis=1, tiled=True)]
    all_to_all x0 -> x1, starting transfers between devices: none -> 8.58 us  [local(): jax.lax.all_to_all(y1, ('dp', 'tensor'), split_axis=0, concat_axis=0)]
  transfers between devices with their start and end apart: 4 -> 5, of which waited for: 2 -> 3; matrix products, arithmetic and copies ran while one was open for 2% -> 2% of each run, Pallas kernels for 0% -> 0%
where the time goes in v1:
time: 473 us; the launch traced here: 472 us
  waiting for transfers between devices  290 us (61%)
  blocking collectives  132 us (28%)
  between operations  21.2 us (4%)
  other arithmetic  13.5 us (3%)
  starting transfers between devices  8.75 us (2%)
  local copies, waits for them, and re-layouts  6.45 us (1%)
    unnamed x5, waiting for transfers between devices  257 us
    psum x1, blocking collectives, local(): lax.psum((jnp.sum(attention_sum * attention_sum), expert_squares, jnp.sum...  79.7 us
    all_gather x1, blocking collectives, local(): lax.all_gather(attention_out[3], 'dp', axis=0, tiled=True)  52.6 us
    reduce_scatter x1, waiting for transfers between devices, local(): lax.psum_scatter(micro_total(expert_local), 'dp', scatter_dimension=1, ti...  24.4 us
  transfers between devices with their start and end apart: 5, of which 3 were waited for; matrix products, arithmetic and copies ran while one was open for 2% of the time, Pallas kernels for 0%

profile of v1, /device:TPU:1, one launch (start us, length us, event | category | flops | bytes accessed | tf_op | source)
XLA Modules:
  0.0 472.4 jit_solution(2244249464418491618)
XLA Ops:
  8.0 0.0 all-reduce.3.cloned.1.call-start
  8.1 1.1 copy.31
  9.1 0.7 bitcast_convert_fusion.2
  9.9 0.0 all-reduce.3.cloned.1.call-update
  9.9 0.0 reduce-scatter.3.cloned.1.call-start
  9.9 2.1 bitcast_convert_fusion.1
  12.1 0.0 reduce-scatter.3.cloned.1.call-update
  12.1 0.0 reduce-scatter.5.cloned.1.call-start
  12.2 2.4 bitcast_convert_fusion
  14.6 0.0 copy-start.8
  14.6 0.0 copy-start.9
  14.6 0.0 copy-start.4
  14.6 0.0 copy-start.6
  14.6 0.0 reduce-scatter.5.cloned.1.call-update
  14.7 0.0 all-gather.2.cloned.1.call-start
  16.8 256.6 %all-reduce.3.cloned.1.call-done = f32[36,512]{0,1:T(8,128)} async-done(((f32[36,512]{0,1:T(8,128)}), f32[36,512]{0,1:T(8,128)}) %all-reduce.3.cloned.1.call-update) | async-done | bytes 73744
  273.4 1.3 multiply_reduce_fusion.1
  274.7 1.3 multiply_reduce_fusion
  276.0 24.4 %reduce-scatter.5.cloned.1.call-done = f32[2,8,1024]{2,1,0:T(8,128)} async-done(((f32[2,512,1024]{2,1,0:T(8,128)}), f32[2,8,1024]{2,1,0:T(8,128)}) %reduce-scatter.5.cloned.1.call-update) | async-done | bytes 65552 | tf_op jit(solution)/shard_map/reduce_scatter | solution.py:52
  300.5 1.4 fusion.1
  304.5 79.7 %psum.25 = f32[]{:T(128)} all-reduce(f32[]{:T(128)S(6)} %add.71), channel_id=1, replica_groups=mesh['dp'=64,'tensor'=4] {'dp','tensor'}, use_global_device_ids=true, to_apply=%region_2.0 | all-reduce | flops 1 | bytes 8 | tf_op jit(solution)/shard_map/psum | solution.py:59
  384.9 1.5 fusion.7
  386.4 0.0 all-gather.2.cloned.1.call-update
  386.5 1.3 fusion.5
  387.8 0.7 stack.2
  388.5 8.6 %all-to-all-start = ((bf16[256,36,2]{1,2,0:T(2,128)(2,1)}), bf16[256,36,2]{1,2,0:T(2,128)(2,1)S(1)}, u32[]{:S(2)}, u32[]{:S(2)}) async-start(bf16[256,36,2]{1,2,0:T(2,128)(2,1)} %stack.2), calls=%async_computation.2 | async-start | bytes 262144 | tf_op jit(solution)/shard_map/all_to_all | solution.py:116
  397.1 1.4 fusion.9
  398.5 52.6 %all_gather.6 = bf16[512,512]{1,0:T(8,128)(2,1)S(1)} all-gather(bf16[8,512]{1,0:T(8,128)(2,1)S(1)} %get-tuple-element.46), channel_id=1, replica_groups=mesh['dp'=64,'tensor'=4] {'dp'}, dimensions={0}, use_global_device_ids=true | all-gather | bytes 532480 | tf_op jit(solution)/shard_map/all_gather | solution.py:84
  451.1 0.7 copy.32
  451.8 9.2 %all-gather.2.cloned.1.call-done = bf16[2,512,1024]{2,1,0:T(8,128)(2,1)} async-done(((bf16[2,8,1024]{2,1,0:T(8,128)(2,1)}), bf16[2,512,1024]{2,1,0:T(8,128)(2,1)}) %all-gather.2.cloned.1.call-update) | async-done | bytes 2097168 | tf_op jit(solution)/shard_map/all_gather | solution.py:98
  461.0 0.8 copy.39
  461.8 3.1 copy.40
  (19 shorter events, 0.0 us)
Async XLA Ops:
  8.0 4.1 copy-start
  8.0 265.4 %all-reduce.3.cloned.1.call-start = ((), (), s32[]{:S(2)}) async-start(), calls=%async_computation.6 | async-start | bytes 524288
  9.9 264.8 %reduce-scatter.3.cloned.1.call-start = ((), (), s32[]{:S(2)}) async-start(), calls=%async_computation.3 | async-start | bytes 1064960 | tf_op jit(solution)/shard_map/reduce_scatter | solution.py:49
  12.1 288.4 %reduce-scatter.5.cloned.1.call-start = ((), (), s32[]{:S(2)}) async-start(), calls=%async_computation.4 | async-start | bytes 4259840 | tf_op jit(solution)/shard_map/reduce_scatter | solution.py:52
  14.6 370.3 %copy-start.1 = (f32[2,8,1024]{2,1,0:T(8,128)S(1)}, f32[2,8,1024]{2,1,0:T(8,128)}, u32[]{:S(2)}) copy-start(f32[2,8,1024]{2,1,0:T(8,128)} %param.21) | copy-start | bytes 196612
  14.6 370.3 %copy-start.2 = (f32[2,8,1024]{2,1,0:T(8,128)S(1)}, f32[2,8,1024]{2,1,0:T(8,128)}, u32[]{:S(2)}) copy-start(f32[2,8,1024]{2,1,0:T(8,128)} %param.23) | copy-start | bytes 196612
  14.6 370.3 %copy-start.3 = (f32[2,8,1024]{2,1,0:T(8,128)S(1)}, f32[2,8,1024]{2,1,0:T(8,128)}, u32[]{:S(2)}) copy-start(f32[2,8,1024]{2,1,0:T(8,128)} %param.22) | copy-start | bytes 196612
  14.6 371.9 %copy-start.7 = (f32[36,2]{0,1:T(2,128)S(1)}, f32[36,2]{0,1:T(2,128)}, u32[]{:S(2)}) copy-start(f32[36,2]{0,1:T(2,128)} %param.24) | copy-start | bytes 868
  14.6 371.9 %copy-start.8 = (f32[36,2]{0,1:T(2,128)S(1)}, f32[36,2]{0,1:T(2,128)}, u32[]{:S(2)}) copy-start(f32[36,2]{0,1:T(2,128)} %param.26) | copy-start | bytes 868
  14.6 371.9 %copy-start.9 = (f32[36,2]{0,1:T(2,128)S(1)}, f32[36,2]{0,1:T(2,128)}, u32[]{:S(2)}) copy-start(f32[36,2]{0,1:T(2,128)} %param.25) | copy-start | bytes 868
  14.6 382.5 %copy-start.4 = (f32[8,512]{1,0:T(8,128)S(1)}, f32[8,512]{1,0:T(8,128)}, u32[]{:S(2)}) copy-start(f32[8,512]{1,0:T(8,128)} %param.18) | copy-start | bytes 49156
  14.6 382.5 %copy-start.5 = (f32[8,512]{1,0:T(8,128)S(1)}, f32[8,512]{1,0:T(8,128)}, u32[]{:S(2)}) copy-start(f32[8,512]{1,0:T(8,128)} %param.20) | copy-start | bytes 49156
  14.6 382.5 %copy-start.6 = (f32[8,512]{1,0:T(8,128)S(1)}, f32[8,512]{1,0:T(8,128)}, u32[]{:S(2)}) copy-start(f32[8,512]{1,0:T(8,128)} %param.19) | copy-start | bytes 49156
  14.7 446.3 %all-gather.2.cloned.1.call-start = ((), (), s32[]{:S(2)}) async-start(), calls=%async_computation.5 | async-start | bytes 2129920 | tf_op jit(solution)/shard_map/all_gather | solution.py:98
  388.5 62.6 %all-to-all-start = ((bf16[256,36,2]{1,2,0:T(2,128)(2,1)}), bf16[256,36,2]{1,2,0:T(2,128)(2,1)S(1)}, u32[]{:S(2)}, u32[]{:S(2)}) async-start(bf16[256,36,2]{1,2,0:T(2,128)(2,1)} %stack.2), calls=%async_computation.2 | async-start | bytes 262144 | tf_op jit(solution)/shard_map/all_to_all | solution.py:116
Sparse Core Ops, SparseCore 0:
  14.9 258.5 all-reduce.2
Sparse Core Ops, SparseCore 1:
  14.9 139.2 reduce-scatter.2
  158.2 142.3 reduce-scatter.4
  386.5 74.4 all-gather.1
